TPU v7x, 256 devices: a whole 4x4x8 slice. The times are simulated.
256 devices in a mesh: people: 2 (over x_hi), tm: 64 (over z, y, core), type: 2 (over x_lo).
Axes of the slice: x: 4 (x_hi: 2, x_lo: 2; x = x_hi * 2 + x_lo), y: 4, z: 8, core: 2. Of those that a mesh axis runs over, the one named last changes fastest.
Arguments:
- features: bfloat16 [3, 2, 16384], P(None, 'people', 'tm'), may hold values from -6 to 6
- wear: int32 [2, 16384], P('people', 'tm'), may hold values 0 or 1
- rec_start: int32 [2], P('people'), may hold values from 0 to 255
- rec_end: int32 [2], P('people'), may hold values from 16129 to 16384
- conv_first: bfloat16 [3, 3, 128], replicated, may hold values from -2 to 2
- conv_second: bfloat16 [3, 128, 128], replicated, may hold values from -0.3125 to 0.3125
- emit_weight: bfloat16 [128, 512], P(None, 'type'), may hold values from -0.5 to 0.5
- leave: float32 [8, 64], P('type'), may hold values from 0.002 to 0.5
- jump: float32 [8, 64, 64], P('type'), may hold values from -6 to 6
- init_logits: float32 [8, 64], P('type'), may hold values from -6 to 6
- type_prior: float32 [8], replicated, may hold values from -4 to 4
Outputs:
- loglik_rate: float32 [2, 8], P('people', 'type')
- type_post: float32 [2, 8], P('people', 'type')
- occupancy: float32 [8, 64], P('type')
- filtered: float32 [2, 16384, 8, 64], P('people', 'tm', 'type')
All inputs are finite; a program needn't handle non-finite values. No bound on the sum of `wear` on one device may be relied on, other than what follows from the above.
Results may differ from a plain program's by a relative error of at most 0.0085.
Values may be sent and summed in bfloat16 or wider, within the bound.
No kernel may reach another device: no remote copies, remote signals or barrier semaphores. Data moves between devices by JAX's collectives and lax.ppermute only.
A program may use at most 64 MiB of HBM per device.

v0:
```python
import jax
import jax.numpy as jnp
from jax import lax
from jax.sharding import PartitionSpec as P

HIGHEST = lax.Precision.HIGHEST
HIGH = lax.Precision.HIGH
TM_SPLIT = (8, 4, 2)
TM = ("tz", "ty", "tc")


def padded(block, sides, width):
    for axis, dim in sides:
        count = 1
        for name in axis:
            count *= lax.axis_size(name)
        forward = [(i, i + 1) for i in range(count - 1)]
        backward = [(target, source) for source, target in forward]
        low = lax.ppermute(
            lax.slice_in_dim(block, block.shape[dim] - width, None, axis=dim), axis, forward
        )
        high = lax.ppermute(lax.slice_in_dim(block, 0, width, axis=dim), axis, backward)
        block = jnp.concatenate([low, block, high], axis=dim)
    return block


def norm_mat(m):
    return m / jnp.sum(m, axis=(-2, -1), keepdims=True)


def norm_vec(v):
    return v / jnp.sum(v, axis=-1, keepdims=True)


def mat_mat(a, b):
    return jnp.einsum("...im,...ml->...il", a, b, precision=HIGH)


def chain(mats):
    while len(mats) > 1:
        half = len(mats) // 2
        left = jnp.stack(mats[0 : 2 * half : 2])
        right = jnp.stack(mats[1 : 2 * half : 2])
        joined = norm_mat(mat_mat(left, right))
        mats = [joined[i] for i in range(half)] + mats[2 * half :]
    return mats[0]


def group_scan(mats, axis, whole=True):
    count = lax.axis_size(axis)
    mine = lax.axis_index(axis)
    eye = jnp.eye(mats.shape[-1], dtype=mats.dtype)
    everyone = lax.all_gather(mats, axis)
    earlier = [jnp.where(mine > j, everyone[j], eye) for j in range(count)]
    if not whole:
        return chain(earlier), None
    both = chain([jnp.stack([earlier[j], everyone[j]]) for j in range(count)])
    return both[0], both[1]


def exclusive_scan(mats, axes):
    parts = []
    for depth, axis in enumerate(reversed(axes)):
        before, mats = group_scan(mats, axis, depth < len(axes) - 1)
        parts.append(before)
    return chain(parts[::-1])


def on_device(
    features,
    wear,
    rec_start,
    rec_end,
    conv_first,
    conv_second,
    emit_weight,
    leave,
    jump,
    init_logits,
    type_prior,
):
    persons = features.shape[1]
    span = features.shape[2]
    kinds = jump.shape[0]
    states = jump.shape[-1]
    tm_index = lax.axis_index(TM)
    type_index = lax.axis_index("type")
    people_index = lax.axis_index("people")
    tm_count = 1
    for axis in TM:
        tm_count *= lax.axis_size(axis)
    total_epochs = span * tm_count
    extended = padded(features, ((TM, 2),), 5)
    first = jnp.zeros((persons, span + 8, conv_first.shape[2]), jnp.float32)
    for tap in range(3):
        first = first + jnp.einsum(
            "ipt,ic->ptc",
            extended[:, :, tap : tap + span + 8],
            conv_first[tap],
            preferred_element_type=jnp.float32,
        )
    wide_pos = tm_index * span - 4 + jnp.arange(span + 8, dtype=jnp.int32)
    inside = (wide_pos >= 0) & (wide_pos < total_epochs)
    first = jnp.where(inside[None, :, None], jax.nn.silu(first), 0.0).astype(jnp.bfloat16)
    second = jnp.zeros((persons, span, conv_second.shape[2]), jnp.float32)
    for tap in range(3):
        second = second + jnp.einsum(
            "ptc,cd->ptd",
            first[:, 4 * tap : 4 * tap + span],
            conv_second[tap],
            preferred_element_type=jnp.float32,
        )
    second = jax.nn.silu(second).astype(jnp.bfloat16)
    logits = jnp.einsum("ptc,cm->ptm", second, emit_weight, preferred_element_type=jnp.float32)
    probs = jnp.exp(jax.nn.log_softmax(logits.reshape(persons, span, kinds, states), axis=-1))
    positions = tm_index * span + jnp.arange(span, dtype=jnp.int32)
    observed = (
        (wear > 0)
        & (positions[None, :] >= rec_start[:, None])
        & (positions[None, :] < rec_end[:, None])
    )
    emis = jnp.where(observed[:, :, None, None], probs, jnp.float32(1.0))
    observed_f = observed.astype(jnp.float32)
    eye_small = jnp.eye(states, dtype=jnp.float32)
    trans = (1.0 - leave)[..., None] * eye_small + leave[..., None] * jax.nn.softmax(jump, axis=-1)
    start = jax.nn.softmax(init_logits, axis=-1)

    pairs = emis.reshape(persons, span // 2, 2, kinds, states)
    e_even = pairs[:, :, 0]
    e_odd = pairs[:, :, 1]
    left = trans[None, None] * e_even[:, :, :, None, :]
    level = jnp.einsum("pjkim,kml->pjkil", left, trans, precision=HIGH) * e_odd[:, :, :, None, :]
    levels = [None, norm_mat(level)]
    while levels[-1].shape[1] > 1:
        last = levels[-1]
        halves = last.reshape((persons, last.shape[1] // 2, 2) + last.shape[2:])
        levels.append(norm_mat(mat_mat(halves[:, :, 0], halves[:, :, 1])))
    device_op = levels[-1][:, 0]

    before = exclusive_scan(device_op, TM)
    alpha_in = norm_vec(jnp.einsum("ki,pkij->pkj", start, before, precision=HIGHEST))

    entry = alpha_in[:, None]
    for depth in range(len(levels) - 1, 1, -1):
        sibling = levels[depth - 1].reshape(
            (persons, entry.shape[1], 2) + levels[depth - 1].shape[2:]
        )[:, :, 0]
        moved = norm_vec(jnp.einsum("pnki,pnkil->pnkl", entry, sibling, precision=HIGHEST))
        entry = jnp.stack([entry, moved], axis=2).reshape(
            persons, 2 * entry.shape[1], kinds, states
        )
    u = jnp.einsum("pjki,kil->pjkl", entry, trans, precision=HIGHEST) * e_even
    c_even = jnp.sum(u, axis=-1)
    a_even = u / c_even[..., None]
    v = jnp.einsum("pjki,kil->pjkl", a_even, trans, precision=HIGHEST) * e_odd
    c_odd = jnp.sum(v, axis=-1)
    a_odd = v / c_odd[..., None]
    filtered = jnp.stack([a_even, a_odd], axis=2).reshape(persons, span, kinds, states)
    own_log = jnp.sum(jnp.log(c_even), axis=1) + jnp.sum(jnp.log(c_odd), axis=1)
    occupied = jnp.einsum("pt,ptks->pks", observed_f, filtered, precision=HIGHEST)
    count = jnp.sum(observed_f, axis=1)

    halves_n = lax.axis_size("type")
    people_n = lax.axis_size("people") * persons
    row = jnp.concatenate(
        [own_log, occupied.reshape(persons, kinds * states), count[:, None]], axis=1
    )
    person_hot = (
        people_index * persons + jnp.arange(persons)[:, None] == jnp.arange(people_n)[None, :]
    ).astype(jnp.float32)
    half_hot = (type_index == jnp.arange(halves_n)).astype(jnp.float32)
    table = person_hot[:, :, None, None] * half_hot[None, None, :, None] * row[:, None, None, :]
    table = jnp.sum(table, axis=0)
    for axis in TM[::-1] + ("people", "type"):
        table = lax.psum(table, axis)

    full = table[:, :, :kinds].reshape(people_n, halves_n * kinds)
    rate_full = full / total_epochs
    post_full = jax.nn.softmax(type_prior[None, :] + 8.0 * rate_full, axis=-1)
    offset = type_index * kinds
    mine = people_index * persons
    rate_own = lax.dynamic_slice(rate_full, (mine, offset), (persons, kinds))
    post_own = lax.dynamic_slice(post_full, (mine, offset), (persons, kinds))
    post_type = lax.dynamic_slice(post_full, (jnp.int32(0), offset), (people_n, kinds))
    occ_all = jnp.take(table, type_index, axis=1)[:, kinds : kinds + kinds * states]
    occ_all = occ_all.reshape(people_n, kinds, states)
    cnt_all = jnp.take(table, type_index, axis=1)[:, kinds + kinds * states]
    numer = jnp.einsum("pk,pks->ks", post_type, occ_all, precision=HIGHEST)
    denom = jnp.einsum("pk,p->k", post_type, cnt_all, precision=HIGHEST)
    occupancy = numer / denom[:, None]
    return (rate_own, post_own, occupancy, filtered)


def solution(mesh):
    people, epochs, halves = mesh.devices.shape
    assert epochs == TM_SPLIT[0] * TM_SPLIT[1] * TM_SPLIT[2]
    fine = jax.sharding.Mesh(
        mesh.devices.reshape((people,) + TM_SPLIT + (halves,)), ("people",) + TM + ("type",)
    )
    return jax.shard_map(
        on_device,
        mesh=fine,
        in_specs=(
            P(None, "people", TM),
            P("people", TM),
            P("people"),
            P("people"),
            P(),
            P(),
            P(None, "type"),
            P("type", None),
            P("type", None, None),
            P("type", None),
            P(),
        ),
        out_specs=(
            P("people", "type"),
            P("people", "type"),
            P("type", None),
            P("people", TM, "type", None),
        ),
        check_vma=False,
    )
```

profile of v0, /device:TPU:4, one launch (start us, length us, event | category | flops | bytes accessed | tf_op | source)
XLA Modules:
  0.0 241.1 jit_solution(17805618320254236789)
XLA Ops:
  1.4 1.7 collective-permute-start
  3.2 1.3 collective-permute-start.1
  6.8 1.2 fusion.143
  18.9 1.1 bitcast_reduce_fusion
  22.0 7.1 %fusion.11 = (f32[128,4]{0,1:T(4,128)S(1)}, f32[4,64,128,64]{2,1,3,0:T(8,128)S(1)}) fusion(f32[128,4,64]{0,2,1:T(8,128)S(1)} %get-tuple-element.53, f32[128,4,64]{0,2,1:T(8,128)S(1)} %get-tuple-element.54, f32[4,64,64]{2,1,0:T(8,128)S(1)} %multiply_add_fusion), kind=kOutput, calls=%fused_computation.14 | convolution fusion | flops 811597312 | bytes 8718336 | tf_op jit(solution)/shard_map/pjkim,kml->pjkil/dot_general | solution.py:132
  29.1 4.3 %fusion.10 = f32[1,128,4,64,64]{1,4,3,2,0:T(8,128)} fusion(f32[4,64,128,64]{2,1,3,0:T(8,128)S(1)} %get-tuple-element.64, f32[128,4]{0,1:T(4,128)S(1)} %get-tuple-element.63, f32[128,4,64]{0,2,1:T(8,128)S(1)} %get-tuple-element.53), kind=kLoop, calls=%fused_computation.13 | loop fusion | flops 4194304 | bytes 16910336 | tf_op jit(solution)/shard_map/div | solution.py:28
  33.4 16.2 %copy.86 = f32[1,128,4,64,64]{4,3,2,1,0:T(8,128)} copy(f32[1,128,4,64,64]{1,4,3,2,0:T(8,128)} %fusion.10) | data formatting | bytes 16777216 | tf_op jit(solution)/shard_map/div | solution.py:28
  49.6 14.2 %fusion.146 = (f32[64,4]{1,0:T(8,128)S(1)}, f32[64,4,64,64]{3,2,1,0:T(8,128)}) fusion(f32[1,64,2,4,64,64]{5,4,3,2,1,0:T(8,128)} %bitcast.470), kind=kOutput, calls=%fused_computation.273 | convolution fusion | flops 403701504 | bytes 12583936 | tf_op jit(solution)/shard_map/...im,...ml->...il/dot_general | solution.py:36
  63.8 4.1 %broadcast_divide_fusion = f32[64,4,64,64]{3,2,1,0:T(8,128)S(1)} fusion(f32[64,4,64,64]{3,2,1,0:T(8,128)} %get-tuple-element.66, f32[64,4]{1,0:T(8,128)S(1)} %get-tuple-element.65), kind=kLoop, calls=%fused_computation.19 | loop fusion | flops 1048576 | bytes 8389632 | tf_op jit(solution)/shard_map/div | solution.py:28
  67.9 3.0 %fusion.147 = (f32[32,4]{1,0:T(8,128)S(1)}, f32[32,4,64,64]{3,2,1,0:T(8,128)S(1)}) fusion(f32[1,32,2,4,64,64]{5,4,3,2,1,0:T(8,128)S(1)} %bitcast.472), kind=kOutput, calls=%fused_computation.274 | convolution fusion | flops 201850752 | bytes 6291968 | tf_op jit(solution)/shard_map/...im,...ml->...il/dot_general | solution.py:36
  71.4 1.3 fusion.148
  75.8 4.1 %all-gather = f32[8,64,64]{2,1,0:T(8,128)S(1)} all-gather(f32[4,64,64]{2,1,0:T(8,128)S(1)} %broadcast_divide_fusion.9), channel_id=2, replica_groups=mesh['people'=2,'tz'=8,'ty'=4,'tc'=2,'type'=2] {'tc'}, dimensions={0}, use_global_device_ids=true | all-gather | bytes 196608 | tf_op jit(solution)/shard_map/all_gather | solution.py:53
  80.5 13.7 %all-gather.1 = f32[4,1,1,4,64,64]{5,4,3,2,1,0:T(8,128)S(1)} all-gather(f32[1,1,1,4,64,64]{5,4,3,2,1,0:T(8,128)S(1)} %slice_bitcast_fusion.59), channel_id=3, replica_groups=mesh['people'=2,'tz'=8,'ty'=4,'tc'=2,'type'=2] {'ty'}, dimensions={0}, use_global_device_ids=true | all-gather | bytes 327680 | tf_op jit(solution)/shard_map/all_gather | solution.py:53
  95.5 32.7 %all-gather.2 = f32[8,1,1,4,64,64]{5,4,3,2,1,0:T(8,128)S(1)} all-gather(f32[1,1,1,4,64,64]{5,4,3,2,1,0:T(8,128)S(1)} %slice_bitcast_fusion.54), channel_id=4, replica_groups=mesh['people'=2,'tz'=8,'ty'=4,'tc'=2,'type'=2] {'tz'}, dimensions={0}, use_global_device_ids=true | all-gather | bytes 589824 | tf_op jit(solution)/shard_map/all_gather | solution.py:53
  131.0 1.1 fusion.92
  132.4 1.3 fusion.69
  136.0 3.5 %fusion.18 = f32[16,4,1,64]{3,2,1,0:T(1,128)S(1)} fusion(f32[1,16,2,4,64,64]{5,4,3,2,1,0:T(8,128)} %bitcast.475, f32[16,4,64,1]{2,0,1,3:T(8,128)S(1)} %bitcast.494), kind=kOutput, calls=%fused_computation.27 | convolution fusion | flops 3145728 | bytes 2129920 | tf_op jit(solution)/shard_map/pnki,pnkil->pnkl/dot_general | solution.py:148
  139.9 5.3 %fusion.16 = f32[32,4,1,64]{3,2,1,0:T(1,128)S(1)} fusion(f32[1,32,2,4,64,64]{5,4,3,2,1,0:T(8,128)} %bitcast.473, f32[32,4,64,1]{2,0,1,3:T(8,128)S(1)} %bitcast.489), kind=kOutput, calls=%fused_computation.22 | convolution fusion | flops 6291456 | bytes 4259840 | tf_op jit(solution)/shard_map/pnki,pnkil->pnkl/dot_general | solution.py:148
  145.7 9.5 %fusion.12 = f32[64,4,1,64]{3,2,1,0:T(1,128)S(1)} fusion(f32[1,64,2,4,64,64]{5,4,3,2,1,0:T(8,128)} %bitcast.471, f32[64,4,64,1]{2,0,1,3:T(8,128)S(1)} %bitcast.484), kind=kOutput, calls=%fused_computation.15 | convolution fusion | flops 12582912 | bytes 8519680 | tf_op jit(solution)/shard_map/pnki,pnkil->pnkl/dot_general | solution.py:148
  158.8 3.9 %psum.35 = f32[2,2,261]{0,2,1:T(8,128)S(1)} all-reduce(f32[2,2,261]{0,2,1:T(8,128)S(1)} %broadcast_multiply_fusion), channel_id=1, replica_groups=mesh['people'=2,'tz'=8,'ty'=4,'tc'=2,'type'=2] {'tc'}, use_global_device_ids=true, to_apply=%region_35.36 | all-reduce | flops 1044 | bytes 8352 | tf_op jit(solution)/shard_map/psum | solution.py:175
  162.8 17.6 %psum.36 = f32[2,2,261]{0,2,1:T(8,128)S(1)} all-reduce(f32[2,2,261]{0,2,1:T(8,128)S(1)} %psum.35), channel_id=1, replica_groups=mesh['people'=2,'tz'=8,'ty'=4,'tc'=2,'type'=2] {'ty'}, use_global_device_ids=true, to_apply=%region_36.37 | all-reduce | flops 1044 | bytes 8352 | tf_op jit(solution)/shard_map/psum | solution.py:175
  180.3 32.0 %psum.37 = f32[2,2,261]{0,2,1:T(8,128)S(1)} all-reduce(f32[2,2,261]{0,2,1:T(8,128)S(1)} %psum.36), channel_id=1, replica_groups=mesh['people'=2,'tz'=8,'ty'=4,'tc'=2,'type'=2] {'tz'}, use_global_device_ids=true, to_apply=%region_37.38 | all-reduce | flops 1044 | bytes 8352 | tf_op jit(solution)/shard_map/psum | solution.py:175
  212.3 13.7 %psum.38 = f32[2,2,261]{0,2,1:T(8,128)S(1)} all-reduce(f32[2,2,261]{0,2,1:T(8,128)S(1)} %psum.37), channel_id=1, replica_groups=mesh['people'=2,'tz'=8,'ty'=4,'tc'=2,'type'=2] {'people'}, use_global_device_ids=true, to_apply=%region_38.39 | all-reduce | flops 1044 | bytes 8352 | tf_op jit(solution)/shard_map/psum | solution.py:175
  226.0 11.2 %psum.39 = f32[2,2,261]{0,2,1:T(8,128)S(1)} all-reduce(f32[2,2,261]{0,2,1:T(8,128)S(1)} %psum.38), channel_id=1, replica_groups=mesh['people'=2,'tz'=8,'ty'=4,'tc'=2,'type'=2] {'type'}, use_global_device_ids=true, to_apply=%region_39.40 | all-reduce | flops 1044 | bytes 8352 | tf_op jit(solution)/shard_map/psum | solution.py:175
  (140 shorter events, 33.3 us)
Async XLA Ops:
  0.6 18.3 %copy-start = (bf16[128,256]{1,0:T(8,128)(2,1)S(1)}, bf16[128,256]{1,0:T(8,128)(2,1)}, u32[]{:S(2)}) copy-start(bf16[128,256]{1,0:T(8,128)(2,1)} %param.19) | copy-start | bytes 196612
  1.4 11.9 %collective-permute-start = (bf16[3,1,5]{2,0,1:T(4,128)(2,1)S(1)}, bf16[3,1,5]{2,0,1:T(4,128)(2,1)S(1)}, u32[]{:S(2)}, u32[]{:S(2)}) collective-permute-start(bf16[3,1,5]{2,0,1:T(4,128)(2,1)S(1)} %get-tuple-element.57), channel_id=1, source_target_pairs={{0,2},{2,4},{4,6},{6,8},{8,10},{10,12},{12,14},{14,16},{16,18},{18... | collective-permute-start | bytes 98 | tf_op jit(solution)/shard_map/ppermute | solution.py:19
  3.2 10.2 %collective-permute-start.1 = (bf16[3,1,5]{2,0,1:T(4,128)(2,1)S(1)}, bf16[3,1,5]{2,0,1:T(4,128)(2,1)S(1)}, u32[]{:S(2)}, u32[]{:S(2)}) collective-permute-start(bf16[3,1,5]{2,0,1:T(4,128)(2,1)S(1)} %get-tuple-element.58), channel_id=1, source_target_pairs={{2,0},{4,2},{6,4},{8,6},{10,8},{12,10},{14,12},{16,14},{18,16},{20... | collective-permute-start | bytes 98 | tf_op jit(solution)/shard_map/ppermute | solution.py:22
  21.3 0.7 copy-start.5
  67.9 3.5 %copy-start.2 = (f32[64,4,64,64]{3,2,1,0:T(8,128)}, f32[64,4,64,64]{3,2,1,0:T(8,128)S(1)}, u32[]{:S(2)}) copy-start(f32[64,4,64,64]{3,2,1,0:T(8,128)S(1)} %broadcast_divide_fusion) | copy-start | bytes 12582916
  71.4 3.0 %copy-start.3 = (f32[32,4,64,64]{3,2,1,0:T(8,128)}, f32[32,4,64,64]{3,2,1,0:T(8,128)S(1)}, u32[]{:S(2)}) copy-start(f32[32,4,64,64]{3,2,1,0:T(8,128)S(1)} %broadcast_divide_fusion.1) | copy-start | bytes 6291460
  74.5 5.9 %copy-start.4 = (f32[4,4,64,64]{3,2,1,0:T(8,128)}, f32[4,4,64,64]{3,2,1,0:T(8,128)S(1)}, u32[]{:S(2)}) copy-start(f32[4,4,64,64]{3,2,1,0:T(8,128)S(1)} %broadcast_divide_fusion.6) | copy-start | bytes 786436
  75.0 0.7 copy-start.7
  136.0 19.9 %copy-start.6 = (f32[1,128,2,4,64]{1,4,3,2,0:T(8,128)S(1)}, f32[1,128,2,4,64]{1,4,3,2,0:T(8,128)}, u32[]{:S(2)}) copy-start(f32[1,128,2,4,64]{1,4,3,2,0:T(8,128)} %copy-done.5) | copy-start | bytes 786436
  145.7 95.4 %copy-start.1 = (bf16[128,256]{1,0:T(8,128)(2,1)S(1)}, bf16[128,256]{1,0:T(8,128)(2,1)}, u32[]{:S(2)}) copy-start(bf16[128,256]{1,0:T(8,128)(2,1)} %param.19) | copy-start | bytes 196612
  145.7 91.8 %copy-start.8 = (f32[8]{0:T(128)S(1)}, f32[8]{0:T(128)}, u32[]{:S(2)}) copy-start(f32[8]{0:T(128)} %param.23) | copy-start | bytes 100
where the time goes:
time: 243 us; the launch traced here: 241 us
  blocking collectives  129 us (53%)
  matrix products  60.7 us (25%)
  local copies, waits for them, and re-layouts  23.6 us (10%)
  other arithmetic  22.3 us (9%)
  starting transfers between devices  3.02 us (1%)
  between operations  2.69 us (1%)
    psum x5, blocking collectives, on_device(): table = lax.psum(table, axis)  78.3 us
    all_gather x3, blocking collectives, group_scan(): everyone = lax.all_gather(mats, axis)  50.5 us
    dot_general x15, matrix products, mat_mat(): return jnp.einsum('...im,...ml->...il', a, b, precision=HIGH)  23.5 us
    dot_general x7, matrix products, on_device(): jnp.einsum('pnki,pnkil->pnkl', entry, sibling, precision=HIGHEST)  22.2 us
    div x1, local copies, waits for them, and re-layouts, norm_mat(): return m / jnp.sum(m, axis=(-2, -1), keepdims=True)  16.2 us
    div x12, other arithmetic, norm_mat(): return m / jnp.sum(m, axis=(-2, -1), keepdims=True)  9.95 us
    dot_general x1, matrix products, on_device(): jnp.einsum('pjkim,kml->pjkil', left, trans, precision=HIGH)  7.06 us
  transfers between devices with their start and end apart: 2, of which 0 were waited for; matrix products, arithmetic and copies ran while one was open for 3% of the time, Pallas kernels for 0%

commit v1 on v0

--- a/solution.py
+++ b/solution.py
@@ -34,6 +34,17 @@
 
 def mat_mat(a, b):
     return jnp.einsum("...im,...ml->...il", a, b, precision=HIGH)
+
+
+def bit_reverse(x, axis):
+    bits = x.shape[axis].bit_length() - 1
+    split = x.shape[:axis] + (2,) * bits + x.shape[axis + 1 :]
+    perm = (
+        list(range(axis))
+        + [axis + bits - 1 - i for i in range(bits)]
+        + list(range(axis + bits, len(split)))
+    )
+    return jnp.transpose(x.reshape(split), perm).reshape(x.shape)
 
 
 def chain(mats):
@@ -125,38 +136,37 @@
     trans = (1.0 - leave)[..., None] * eye_small + leave[..., None] * jax.nn.softmax(jump, axis=-1)
     start = jax.nn.softmax(init_logits, axis=-1)
 
-    pairs = emis.reshape(persons, span // 2, 2, kinds, states)
-    e_even = pairs[:, :, 0]
-    e_odd = pairs[:, :, 1]
-    left = trans[None, None] * e_even[:, :, :, None, :]
-    level = jnp.einsum("pjkim,kml->pjkil", left, trans, precision=HIGH) * e_odd[:, :, :, None, :]
+    order = bit_reverse(jnp.transpose(emis, (2, 0, 1, 3)), 2)
+    half = span // 2
+    e_even = order[:, :, :half]
+    e_odd = order[:, :, half:]
+    left = trans[:, None, None] * e_even[:, :, :, None, :]
+    level = jnp.einsum("kpjim,kml->kpjil", left, trans, precision=HIGH) * e_odd[:, :, :, None, :]
     levels = [None, norm_mat(level)]
-    while levels[-1].shape[1] > 1:
+    while levels[-1].shape[2] > 1:
         last = levels[-1]
-        halves = last.reshape((persons, last.shape[1] // 2, 2) + last.shape[2:])
-        levels.append(norm_mat(mat_mat(halves[:, :, 0], halves[:, :, 1])))
-    device_op = levels[-1][:, 0]
+        n = last.shape[2] // 2
+        levels.append(norm_mat(mat_mat(last[:, :, :n], last[:, :, n:])))
+    device_op = levels[-1][:, :, 0]
 
     before = exclusive_scan(device_op, TM)
-    alpha_in = norm_vec(jnp.einsum("ki,pkij->pkj", start, before, precision=HIGHEST))
-
-    entry = alpha_in[:, None]
+    alpha_in = norm_vec(jnp.einsum("ki,kpij->kpj", start, before, precision=HIGHEST))
+
+    entry = alpha_in[:, :, None]
     for depth in range(len(levels) - 1, 1, -1):
-        sibling = levels[depth - 1].reshape(
-            (persons, entry.shape[1], 2) + levels[depth - 1].shape[2:]
-        )[:, :, 0]
-        moved = norm_vec(jnp.einsum("pnki,pnkil->pnkl", entry, sibling, precision=HIGHEST))
-        entry = jnp.stack([entry, moved], axis=2).reshape(
-            persons, 2 * entry.shape[1], kinds, states
-        )
-    u = jnp.einsum("pjki,kil->pjkl", entry, trans, precision=HIGHEST) * e_even
+        n = entry.shape[2]
+        sibling = levels[depth - 1][:, :, :n]
+        moved = norm_vec(jnp.einsum("kpni,kpnil->kpnl", entry, sibling, precision=HIGHEST))
+        entry = jnp.concatenate([entry, moved], axis=2)
+    u = jnp.einsum("kpji,kil->kpjl", entry, trans, precision=HIGHEST) * e_even
     c_even = jnp.sum(u, axis=-1)
     a_even = u / c_even[..., None]
-    v = jnp.einsum("pjki,kil->pjkl", a_even, trans, precision=HIGHEST) * e_odd
+    v = jnp.einsum("kpji,kil->kpjl", a_even, trans, precision=HIGHEST) * e_odd
     c_odd = jnp.sum(v, axis=-1)
     a_odd = v / c_odd[..., None]
-    filtered = jnp.stack([a_even, a_odd], axis=2).reshape(persons, span, kinds, states)
-    own_log = jnp.sum(jnp.log(c_even), axis=1) + jnp.sum(jnp.log(c_odd), axis=1)
+    alpha = bit_reverse(jnp.concatenate([a_even, a_odd], axis=2), 2)
+    filtered = jnp.transpose(alpha, (1, 2, 0, 3))
+    own_log = jnp.transpose(jnp.sum(jnp.log(c_even), axis=2) + jnp.sum(jnp.log(c_odd), axis=2))
     occupied = jnp.einsum("pt,ptks->pks", observed_f, filtered, precision=HIGHEST)
     count = jnp.sum(observed_f, axis=1)
 
@@ -171,7 +181,7 @@
     half_hot = (type_index == jnp.arange(halves_n)).astype(jnp.float32)
     table = person_hot[:, :, None, None] * half_hot[None, None, :, None] * row[:, None, None, :]
     table = jnp.sum(table, axis=0)
-    for axis in TM[::-1] + ("people", "type"):
+    for axis in TM[::-1] + (("people", "type"),):
         table = lax.psum(table, axis)
 
     full = table[:, :, :kinds].reshape(people_n, halves_n * kinds)

time: 243 us -> 243 us (level)
  matrix products: 60.7 us -> 45.8 us
  local copies, waits for them, and re-layouts: 23.6 us -> 37.8 us
  blocking collectives: 129 us -> 122 us
  other arithmetic: 22.3 us -> 28.9 us
    another operation x7 -> x3, local copies, waits for them, and re-layouts: 0.67 us -> 25.1 us  [the longest x6 0.42 us: on_device(): jnp.stack([entry, moved], axis=2)]
    dot_general x11 -> x9, matrix products: 30.6 us -> 15.7 us  [the longest x1 7.32 us: on_device(): jnp.einsum('kpjim,kml->kpjil', left, trans, precision=HIGH)]
    div x1 -> x4, local copies, waits for them, and re-layouts: 16.2 us -> 1.96 us  [norm_vec(): return v / jnp.sum(v, axis=-1, keepdims=True)]
    psum x5 -> x4, blocking collectives: 78.3 us -> 71.5 us  [on_device(): table = lax.psum(table, axis)]
    dot_general x0 -> x1, other arithmetic: none -> 4.59 us  [on_device(): jnp.einsum('kpni,kpnil->kpnl', entry, sibling, precision=HIGHEST)]
    unnamed x0 -> x1, other arithmetic: none -> 2.92 us
    div x12 -> x13, other arithmetic: 9.95 us -> 7.82 us  [norm_mat(): return m / jnp.sum(m, axis=(-2, -1), keepdims=True)]
where the time goes in v1:
time: 243 us; the launch traced here: 240 us
  blocking collectives  122 us (50%)
  matrix products  45.8 us (19%)
  local copies, waits for them, and re-layouts  37.8 us (16%)
  other arithmetic  28.9 us (12%)
  starting transfers between devices  3.02 us (1%)
  between operations  2.74 us (1%)
    psum x4, blocking collectives, on_device(): table = lax.psum(table, axis)  71.5 us
    all_gather x3, blocking collectives, group_scan(): everyone = lax.all_gather(mats, axis)  50.5 us
    another operation x3, local copies, waits for them, and re-layouts  25.1 us
    dot_general x15, matrix products, mat_mat(): return jnp.einsum('...im,...ml->...il', a, b, precision=HIGH)  23.6 us
    div x13, other arithmetic, norm_mat(): return m / jnp.sum(m, axis=(-2, -1), keepdims=True)  7.82 us
    dot_general x1, matrix products, on_device(): jnp.einsum('kpjim,kml->kpjil', left, trans, precision=HIGH)  7.32 us
    dot_general x5, matrix products, on_device(): jnp.einsum('kpni,kpnil->kpnl', entry, sibling, precision=HIGHEST)  7.3 us
  transfers between devices with their start and end apart: 2, of which 0 were waited for; matrix products, arithmetic and copies ran while one was open for 3% of the time, Pallas kernels for 0%

profile of v1, /device:TPU:4, one launch (start us, length us, event | category | flops | bytes accessed | tf_op | source)
XLA Modules:
  0.0 240.3 jit_solution(10083057983494404153)
XLA Ops:
  1.4 1.7 collective-permute-start
  3.2 1.3 collective-permute-start.1
  21.5 7.3 %multiply_reduce_fusion.1 = (f32[4,128]{1,0:T(4,128)S(1)}, f32[4,128,64,64]{1,3,2,0:T(8,128)S(1)}) fusion(f32[4,128,64]{1,2,0:T(8,128)S(1)} %bitcast.450, f32[4,64,64]{2,1,0:T(8,128)S(1)} %multiply_add_fusion, f32[4,128,64]{1,2,0:T(8,128)S(1)} %bitcast.455), kind=kOutput, calls=%fused_computation.13 | convolution fusion | flops 811597312 | bytes 8718336 | tf_op jit(solution)/shard_map/kpjim,kml->kpjil/dot_general | solution.py:144
  28.8 2.0 divide_bitcast_fusion.1
  30.9 7.6 %slice_bitcast_fusion = (f32[4,64,64,64]{1,3,2,0:T(8,128)}, f32[4,64,64,64]{1,3,2,0:T(8,128)}) fusion(f32[4,1,128,64,64]{2,4,3,0,1:T(8,128)S(1)} %divide_bitcast_fusion.1), kind=kLoop, calls=%fused_computation.6 | loop fusion | bytes 16777216 | tf_op jit(solution)/shard_map/reshape.45
  39.1 8.7 %copy.88 = f32[4,64,64,64]{3,2,1,0:T(8,128)} copy(f32[4,64,64,64]{1,3,2,0:T(8,128)} %get-tuple-element.31) | data formatting | bytes 8388608 | tf_op jit(solution)/shard_map/reshape.44
  47.9 8.7 %copy.89 = f32[4,64,64,64]{3,2,1,0:T(8,128)} copy(f32[4,64,64,64]{1,3,2,0:T(8,128)} %get-tuple-element.30) | data formatting | bytes 8388608 | tf_op jit(solution)/shard_map/reshape.45
  56.6 14.1 %fusion.131 = (f32[4,64]{1,0:T(4,128)S(1)}, f32[4,64,64,64]{3,2,1,0:T(8,128)}) fusion(f32[4,64,64,64]{3,2,1,0:T(8,128)} %copy.88, f32[4,64,64,64]{3,2,1,0:T(8,128)} %copy.89), kind=kOutput, calls=%fused_computation.256 | convolution fusion | flops 403701504 | bytes 12583936 | tf_op jit(solution)/shard_map/...im,...ml->...il/dot_general | solution.py:36
  70.7 4.1 %divide_bitcast_fusion = f32[4,1,64,64,64]{4,3,2,0,1:T(8,128)S(1)} fusion(f32[4,64,64,64]{3,2,1,0:T(8,128)} %get-tuple-element.70, f32[4,64]{1,0:T(4,128)S(1)} %get-tuple-element.69), kind=kLoop, calls=%fused_computation.9 | loop fusion | flops 1048576 | bytes 8389632 | tf_op jit(solution)/shard_map/div | solution.py:28
  74.9 3.1 %fusion.132 = (f32[4,32]{1,0:T(4,128)S(1)}, f32[4,32,64,64]{3,2,1,0:T(8,128)S(1)}) fusion(f32[4,1,64,64,64]{4,3,2,0,1:T(8,128)S(1)} %divide_bitcast_fusion), kind=kOutput, calls=%fused_computation.257 | convolution fusion | flops 201850752 | bytes 6291968 | tf_op jit(solution)/shard_map/...im,...ml->...il/dot_general | solution.py:36
  78.5 1.4 fusion.133
  82.9 4.1 %all-gather = f32[8,64,64]{2,1,0:T(8,128)S(1)} all-gather(f32[4,64,64]{2,1,0:T(8,128)S(1)} %broadcast_divide_fusion.5), channel_id=2, replica_groups=mesh['people'=2,'tz'=8,'ty'=4,'tc'=2,'type'=2] {'tc'}, dimensions={0}, use_global_device_ids=true | all-gather | bytes 196608 | tf_op jit(solution)/shard_map/all_gather | solution.py:64
  87.5 13.7 %all-gather.1 = f32[4,1,4,1,64,64]{5,4,3,2,1,0:T(8,128)S(1)} all-gather(f32[1,1,4,1,64,64]{5,4,3,2,1,0:T(8,128)S(1)} %slice_bitcast_fusion.55), channel_id=3, replica_groups=mesh['people'=2,'tz'=8,'ty'=4,'tc'=2,'type'=2] {'ty'}, dimensions={0}, use_global_device_ids=true | all-gather | bytes 327680 | tf_op jit(solution)/shard_map/all_gather | solution.py:64
  102.5 32.7 %all-gather.2 = f32[8,1,4,1,64,64]{5,4,3,2,1,0:T(8,128)S(1)} all-gather(f32[1,1,4,1,64,64]{5,4,3,2,1,0:T(8,128)S(1)} %slice_bitcast_fusion.50), channel_id=4, replica_groups=mesh['people'=2,'tz'=8,'ty'=4,'tc'=2,'type'=2] {'tz'}, dimensions={0}, use_global_device_ids=true | all-gather | bytes 589824 | tf_op jit(solution)/shard_map/all_gather | solution.py:64
  141.0 1.3 fusion.61
  143.1 1.6 fusion.23
  148.2 3.4 %fusion.12 = f32[4,16,1,64]{3,2,1,0:T(1,128)S(1)} fusion(f32[4,16,64,1]{2,3,1,0:T(1,128)S(1)} %bitcast.461, f32[4,1,32,64,64]{4,3,2,0,1:T(8,128)} %copy-done.4), kind=kOutput, calls=%fused_computation.25 | convolution fusion | flops 3145728 | bytes 2129920 | tf_op jit(solution)/shard_map/kpni,kpnil->kpnl/dot_general | solution.py:159
  151.8 1.3 concatenate.41
  153.2 2.9 %multiply_reduce_fusion.2 = f32[4,32,64]{2,1,0:T(8,128)S(1)} fusion(f32[4,1,64,64,64]{4,3,2,0,1:T(8,128)} %copy-done.3, f32[4,32,64]{2,1,0:T(8,128)S(1)} %copy.164), kind=kLoop, calls=%fused_computation.17 | loop fusion | flops 1040384 | bytes 2162688
  156.7 4.6 %multiply_reduce_fusion = f32[4,64,64]{1,2,0:T(8,128)S(1)} fusion(f32[4,64,64]{1,2,0:T(8,128)S(1)} %bitcast.457, f32[4,1,128,64,64]{2,4,3,0,1:T(8,128)} %copy-done.2), kind=kLoop, calls=%fused_computation.8 | loop fusion | flops 2080768 | bytes 4325376 | tf_op jit(solution)/shard_map/kpni,kpnil->kpnl/dot_general | solution.py:159
  164.8 3.9 %psum.28 = f32[2,2,261]{0,2,1:T(8,128)S(1)} all-reduce(f32[2,2,261]{0,2,1:T(8,128)S(1)} %broadcast_multiply_fusion), channel_id=1, replica_groups=mesh['people'=2,'tz'=8,'ty'=4,'tc'=2,'type'=2] {'tc'}, use_global_device_ids=true, to_apply=%region_35.36 | all-reduce | flops 1044 | bytes 8352 | tf_op jit(solution)/shard_map/psum | solution.py:185
  168.7 17.6 %psum.29 = f32[2,2,261]{0,2,1:T(8,128)S(1)} all-reduce(f32[2,2,261]{0,2,1:T(8,128)S(1)} %psum.28), channel_id=1, replica_groups=mesh['people'=2,'tz'=8,'ty'=4,'tc'=2,'type'=2] {'ty'}, use_global_device_ids=true, to_apply=%region_36.37 | all-reduce | flops 1044 | bytes 8352 | tf_op jit(solution)/shard_map/psum | solution.py:185
  186.3 32.2 %psum.30 = f32[2,2,261]{0,2,1:T(8,128)S(1)} all-reduce(f32[2,2,261]{0,2,1:T(8,128)S(1)} %psum.29), channel_id=1, replica_groups=mesh['people'=2,'tz'=8,'ty'=4,'tc'=2,'type'=2] {'tz'}, use_global_device_ids=true, to_apply=%region_37.38 | all-reduce | flops 1044 | bytes 8352 | tf_op jit(solution)/shard_map/psum | solution.py:185
  218.5 17.9 %psum.31 = f32[2,2,261]{0,2,1:T(8,128)S(1)} all-reduce(f32[2,2,261]{0,2,1:T(8,128)S(1)} %psum.30), channel_id=1, replica_groups=mesh['people'=2,'tz'=8,'ty'=4,'tc'=2,'type'=2] {'people','type'}, use_global_device_ids=true, to_apply=%region_38.39 | all-reduce | flops 1044 | bytes 8352 | tf_op jit(solution)/shard_map/psum | solution.py:185
  (152 shorter events, 40.3 us)
Async XLA Ops:
  0.6 18.0 %copy-start = (bf16[128,256]{1,0:T(8,128)(2,1)S(1)}, bf16[128,256]{1,0:T(8,128)(2,1)}, u32[]{:S(2)}) copy-start(bf16[128,256]{1,0:T(8,128)(2,1)} %param.19) | copy-start | bytes 196612
  1.4 11.7 %collective-permute-start = (bf16[3,1,5]{2,0,1:T(4,128)(2,1)S(1)}, bf16[3,1,5]{2,0,1:T(4,128)(2,1)S(1)}, u32[]{:S(2)}, u32[]{:S(2)}) collective-permute-start(bf16[3,1,5]{2,0,1:T(4,128)(2,1)S(1)} %get-tuple-element.61), channel_id=1, source_target_pairs={{0,2},{2,4},{4,6},{6,8},{8,10},{10,12},{12,14},{14,16},{16,18},{18... | collective-permute-start | bytes 98 | tf_op jit(solution)/shard_map/ppermute | solution.py:19
  3.2 10.0 %collective-permute-start.1 = (bf16[3,1,5]{2,0,1:T(4,128)(2,1)S(1)}, bf16[3,1,5]{2,0,1:T(4,128)(2,1)S(1)}, u32[]{:S(2)}, u32[]{:S(2)}) collective-permute-start(bf16[3,1,5]{2,0,1:T(4,128)(2,1)S(1)} %get-tuple-element.62), channel_id=1, source_target_pairs={{2,0},{4,2},{6,4},{8,6},{10,8},{12,10},{14,12},{16,14},{18,16},{20... | collective-permute-start | bytes 98 | tf_op jit(solution)/shard_map/ppermute | solution.py:22
  21.4 9.5 %copy-start.10 = (f32[4,1,128,64]{2,3,0,1:T(8,128)}, f32[4,1,128,64]{2,3,0,1:T(8,128)S(1)}, u32[]{:S(2)}) copy-start(f32[4,1,128,64]{2,3,0,1:T(8,128)S(1)} %copy.161) | copy-start | bytes 393220
  30.9 8.3 %copy-start.2 = (f32[4,1,128,64,64]{2,4,3,0,1:T(8,128)}, f32[4,1,128,64,64]{2,4,3,0,1:T(8,128)S(1)}, u32[]{:S(2)}) copy-start(f32[4,1,128,64,64]{2,4,3,0,1:T(8,128)S(1)} %divide_bitcast_fusion.1) | copy-start | bytes 25165828
  74.9 3.6 %copy-start.3 = (f32[4,1,64,64,64]{4,3,2,0,1:T(8,128)}, f32[4,1,64,64,64]{4,3,2,0,1:T(8,128)S(1)}, u32[]{:S(2)}) copy-start(f32[4,1,64,64,64]{4,3,2,0,1:T(8,128)S(1)} %divide_bitcast_fusion) | copy-start | bytes 12582916
  78.5 3.0 %copy-start.4 = (f32[4,1,32,64,64]{4,3,2,0,1:T(8,128)}, f32[4,1,32,64,64]{4,3,2,0,1:T(8,128)S(1)}, u32[]{:S(2)}) copy-start(f32[4,1,32,64,64]{4,3,2,0,1:T(8,128)S(1)} %divide_bitcast_fusion.2) | copy-start | bytes 6291460
  81.6 5.9 %copy-start.5 = (f32[4,1,4,64,64]{4,3,2,0,1:T(8,128)}, f32[4,1,4,64,64]{4,3,2,0,1:T(8,128)S(1)}, u32[]{:S(2)}) copy-start(f32[4,1,4,64,64]{4,3,2,0,1:T(8,128)S(1)} %divide_bitcast_fusion.5) | copy-start | bytes 786436
  82.1 0.7 copy-start.9
  146.2 10.2 %copy-start.6 = (f32[4,1,1,64]{2,3,0,1:T(8,128)S(1)}, f32[4,1,1,64]{2,3,0,1:T(8,128)}, u32[]{:S(2)}) copy-start(f32[4,1,1,64]{2,3,0,1:T(8,128)} %copy.121) | copy-start | bytes 3076
  146.2 10.2 %copy-start.7 = (f32[4,1,1,64]{2,3,0,1:T(8,128)S(1)}, f32[4,1,1,64]{2,3,0,1:T(8,128)}, u32[]{:S(2)}) copy-start(f32[4,1,1,64]{2,3,0,1:T(8,128)} %copy.120) | copy-start | bytes 3076
  146.2 10.2 %copy-start.8 = (f32[4,1,2,64]{2,3,0,1:T(8,128)S(1)}, f32[4,1,2,64]{2,3,0,1:T(8,128)}, u32[]{:S(2)}) copy-start(f32[4,1,2,64]{2,3,0,1:T(8,128)} %fusion.23) | copy-start | bytes 6148
  153.1 8.6 %copy-start.11 = (f32[4,1,128,64]{2,3,0,1:T(8,128)S(1)}, f32[4,1,128,64]{2,3,0,1:T(8,128)}, u32[]{:S(2)}) copy-start(f32[4,1,128,64]{2,3,0,1:T(8,128)} %copy-done.10) | copy-start | bytes 393220
  156.7 83.6 %copy-start.1 = (bf16[128,256]{1,0:T(8,128)(2,1)S(1)}, bf16[128,256]{1,0:T(8,128)(2,1)}, u32[]{:S(2)}) copy-start(bf16[128,256]{1,0:T(8,128)(2,1)} %param.19) | copy-start | bytes 196612
  156.7 80.0 %copy-start.12 = (f32[8]{0:T(128)S(1)}, f32[8]{0:T(128)}, u32[]{:S(2)}) copy-start(f32[8]{0:T(128)} %param.23) | copy-start | bytes 100
